TPU v7x, 512 devices: a whole 4x8x8 slice. The times are simulated.
512 devices in a mesh: grp: 64 (over z_hi, y, core), mdl: 8 (over z_lo, x).
Axes of the slice: x: 4, y: 8, z: 8 (z_hi: 4, z_lo: 2; z = z_hi * 2 + z_lo), core: 2. Of those that a mesh axis runs over, the one named last changes fastest.
Arguments:
- draft_hidden: bfloat16 [128, 32, 2048], P('grp', None, 'mdl'), may hold values from -6 to 6
- q_weight: bfloat16 [4, 2048, 1024], P(None, None, 'mdl'), may hold values from -0.125 to 0.125
- kv_weight: bfloat16 [2, 2048, 1024], P(None, None, 'mdl'), may hold values from -0.125 to 0.125
- router_weight: float32 [2048, 4], replicated, may hold values from -0.125 to 0.125
- routes: int32 [128, 32, 2], P('grp'), may hold values from 0 to 3, all different within a row
- tree_mask: int32 [128, 32, 32], P('grp'), may hold values from 0 to 1, as said below
- accepted: int32 [128, 8], P('grp'), may hold values from 0 to 31, as said below
- cache_kv: bfloat16 [192, 2, 1024, 1024], P('grp', None, None, 'mdl')
- cache_len: int32 [192], P('grp'), may hold values from 1 to 1024
- slot_request: int32 [192], replicated, may hold values from 0 to 127, as said below
Outputs:
- verified: bfloat16 [128, 8, 2, 1024], P('grp', None, None, 'mdl')
Inputs may be any that keep to these rules, and one draw needn't show every extreme that they name: `routes`: the 2 experts of one token differ. tree_mask[r, i, j] is 1 exactly when draft j is draft i or an ancestor of it; every draft's parent has a lower index and draft 0 is the root. `accepted`: each row holds the first 8 drafts of the root-to-node chain of one draft, in increasing order; a shorter chain is followed by repeats of its last draft. `slot_request`: the requests of one index of grp are the 2 in a row that it holds; they are served by 3 slots in all, 1 of them by two slots and the others by one; no index of grp holds more than 1 slot serving requests of any one index of grp, and some pairs of indices have exactly 1 such slot.
All inputs are finite; a program needn't handle non-finite values.
Results may differ from a plain program's by a relative error of at most 0.014.
The roundings to bfloat16 on the way count: a program that leaves them out, or rounds other values in their place, can miss the bound.
Values may be sent and summed in bfloat16 or wider, within the bound.
No kernel may reach another device: no remote copies, remote signals or barrier semaphores. Data moves between devices by JAX's collectives and lax.ppermute only.
A program may use at most 64 MiB of HBM per device.

v0:
```python
import jax
import jax.numpy as jnp
from jax import lax
from jax.sharding import PartitionSpec as P

HEAD_SIZE = 128


def softmax_piece(scores, usable, values, contract):
    masked = jnp.where(usable, scores, -jnp.inf)
    peak_score = jnp.max(masked, axis=-1)
    weights_low = jnp.exp(masked - peak_score[..., None]).astype(jnp.bfloat16)
    denominator = jnp.sum(weights_low.astype(jnp.float32), axis=-1)
    numerator = jnp.einsum(contract, weights_low, values, preferred_element_type=jnp.float32)
    return (peak_score, denominator, numerator)


def blend(running, pieces, matched):
    running_max, denominator, numerator = running
    piece_peak, piece_den, piece_num = pieces
    candidate = jnp.where(matched[:, :, None, None, None], piece_peak[None], -jnp.inf)
    new_max = jnp.maximum(running_max, jnp.max(candidate, axis=1))
    rescale = jnp.exp(running_max - new_max)
    weight = jnp.exp(candidate - new_max[:, None])
    denominator = denominator * rescale + jnp.sum(weight * piece_den[None], axis=1)
    numerator = numerator * rescale[..., None] + jnp.einsum(
        "rnqkh,nqkhd->rqkhd", weight, piece_num, precision=lax.Precision.HIGHEST
    )
    return (new_max, denominator, numerator)


def on_device(
    draft_hidden,
    q_weight,
    kv_weight,
    router_weight,
    routes,
    tree_mask,
    accepted,
    cache_kv,
    cache_len,
    slot_request,
):
    highest = lax.Precision.HIGHEST
    requests, drafts, part_width = draft_hidden.shape
    experts = q_weight.shape[0]
    head_width = q_weight.shape[2]
    head_count = head_width // HEAD_SIZE
    topk_count = routes.shape[2]
    row_count = requests * drafts
    score_scale = HEAD_SIZE ** (-0.5)
    pieces = lax.all_gather(draft_hidden, "mdl", axis=2, tiled=True)
    piece_size = pieces.shape[2]
    piece_rows = pieces.reshape(row_count, piece_size)
    q_sum = jnp.einsum("nd,edw->new", piece_rows, q_weight, preferred_element_type=jnp.float32)
    kv_sum = jnp.einsum("nd,cdw->ncw", piece_rows, kv_weight, preferred_element_type=jnp.float32)
    logit_sum = jnp.dot(piece_rows.astype(jnp.float32), router_weight, precision=highest)
    route_flat = routes.reshape(row_count, topk_count)
    chosen_mask = route_flat[:, :, None] == jnp.arange(experts, dtype=jnp.int32)[None, None, :]
    chosen = jnp.sum(jnp.where(chosen_mask, logit_sum[:, None, :], 0.0), axis=2)
    gate_probs = jax.nn.softmax(chosen, axis=-1).reshape(requests, drafts, topk_count)
    queries = jnp.sum(jnp.where(chosen_mask[:, :, :, None], q_sum[:, None], 0.0), axis=2)
    queries = queries.astype(jnp.bfloat16).reshape(
        requests, drafts, topk_count, head_count, HEAD_SIZE
    )
    draft_keys = kv_sum[:, 0].astype(jnp.bfloat16).reshape(requests, drafts, head_count, HEAD_SIZE)
    draft_values = (
        kv_sum[:, 1].astype(jnp.bfloat16).reshape(requests, drafts, head_count, HEAD_SIZE)
    )
    query_len = queries.shape[1]
    tree_scores = (
        jnp.einsum("rqkhd,rjhd->rqkhj", queries, draft_keys, preferred_element_type=jnp.float32)
        * score_scale
    )
    allowed = (tree_mask > 0)[:, :, None, None, :]
    tree_peak, tree_den, tree_num = softmax_piece(
        tree_scores, allowed, draft_values, "rqkhj,rjhd->rqkhd"
    )
    slot_count = cache_kv.shape[0]
    cache_size = cache_kv.shape[2]
    group_idx = lax.axis_index("grp")
    sending = queries.reshape(requests, query_len, topk_count * head_width)
    my_requests = lax.dynamic_slice_in_dim(slot_request, group_idx * slot_count, slot_count)
    pieces = lax.all_gather(sending, "grp", axis=0, tiled=True)
    piece_count = pieces.shape[0]
    selector = (my_requests[:, None] == jnp.arange(piece_count, dtype=jnp.int32)[None, :]).astype(
        jnp.bfloat16
    )
    slot_queries = jnp.einsum(
        "sn,nqw->sqw", selector, pieces, preferred_element_type=jnp.float32
    ).astype(jnp.bfloat16)
    slot_queries = slot_queries.reshape(slot_count, query_len, topk_count, head_count, HEAD_SIZE)
    cache_keys = cache_kv[:, 0].reshape(slot_count, cache_size, head_count, HEAD_SIZE)
    cache_values = cache_kv[:, 1].reshape(slot_count, cache_size, head_count, HEAD_SIZE)
    slot_scores = (
        jnp.einsum(
            "sqkhd,schd->sqkhc", slot_queries, cache_keys, preferred_element_type=jnp.float32
        )
        * score_scale
    )
    in_cache = (jnp.arange(cache_size, dtype=jnp.int32)[None, :] < cache_len[:, None])[
        :, None, None, None, :
    ]
    slot_peak, slot_den, slot_num = softmax_piece(
        slot_scores, in_cache, cache_values, "sqkhc,schd->sqkhd"
    )
    home_ids = group_idx * requests + jnp.arange(requests, dtype=jnp.int32)
    pieces = (
        lax.all_gather(slot_peak, "grp", axis=0, tiled=True),
        lax.all_gather(slot_den, "grp", axis=0, tiled=True),
        lax.all_gather(slot_num, "grp", axis=0, tiled=True),
    )
    running_max, denominator, numerator = blend(
        (tree_peak, tree_den, tree_num), pieces, home_ids[:, None] == slot_request[None, :]
    )
    final_num = jnp.take_along_axis(numerator, accepted[:, :, None, None, None], axis=1)
    final_den = jnp.take_along_axis(denominator, accepted[:, :, None, None], axis=1)
    final_gate = jnp.take_along_axis(gate_probs, accepted[:, :, None], axis=1)
    mixed = final_gate[:, :, :, None, None] * final_num / final_den[..., None]
    kept_rows = accepted.shape[1]
    return mixed.reshape(requests, kept_rows, topk_count, head_width).astype(jnp.bfloat16)


def solution(mesh):
    in_specs = (
        P("grp", None, "mdl"),
        P(None, None, "mdl"),
        P(None, None, "mdl"),
        P(),
        P("grp", None, None),
        P("grp", None, None),
        P("grp", None),
        P("grp", None, None, "mdl"),
        P("grp"),
        P(),
    )
    out_specs = P("grp", None, None, "mdl")
    return jax.shard_map(
        on_device, mesh=mesh, in_specs=in_specs, out_specs=out_specs, check_vma=False
    )
```

profile of v0, /device:TPU:1, one launch (start us, length us, event | category | flops | bytes accessed | tf_op | source)
XLA Modules:
  0.0 317.8 jit_solution(7277483683072777976)
XLA Ops:
  6.5 0.8 copy.87
  7.5 24.4 %all_gather.15 = bf16[2,32,2048]{2,1,0:T(8,128)(2,1)S(1)} all-gather(bf16[2,32,256]{2,1,0:T(8,128)(2,1)} %param.10), channel_id=1, replica_groups=mesh['grp'=64,'mdl'=8] {'mdl'}, dimensions={2}, use_global_device_ids=true | all-gather | bytes 294912 | tf_op jit(solution)/shard_map/all_gather | solution.py:52
  31.9 0.5 fusion.48
  32.4 0.1 select_reduce_fusion
  32.6 0.6 convert_element_type.49
  33.4 94.7 %all-gather.5.cloned.1.call-done = bf16[128,32,256]{2,1,0:T(8,128)(2,1)} async-done(((bf16[2,32,256]{2,1,0:T(8,128)(2,1)}), bf16[128,32,256]{2,1,0:T(8,128)(2,1)}) %all-gather.5.cloned.1.call-update) | async-done | bytes 2097168 | tf_op jit(solution)/shard_map/all_gather | solution.py:84
  128.1 2.8 fusion.8
  131.0 1.6 fusion.45
  132.6 2.1 convolution_bitcast_fusion
  134.8 0.1 copy.91
  134.9 0.3 fusion.47
  135.3 0.1 copy.116
  135.6 0.1 exponential_divide_fusion
  135.7 0.6 gather_fusion
  136.4 1.5 convolution_convert_fusion
  138.0 0.2 fusion.46
  138.3 80.5 %all-gather = f32[192,32,2]{1,2,0:T(2,128)S(1)} all-gather(f32[3,32,2]{1,2,0:T(2,128)S(1)} %get-tuple-element.11), channel_id=2, replica_groups=mesh['grp'=64,'mdl'=8] {'grp'}, dimensions={0}, use_global_device_ids=true | all-gather | bytes 49920 | tf_op jit(solution)/shard_map/all_gather | solution.py:109
  218.8 0.1 copy.99
  218.9 0.1 copy.103
  219.0 0.1 select_reduce_fusion.1
  219.1 0.1 copy.104
  219.2 0.3 convert_reduce_fusion
  219.5 77.0 %all-gather.1 = f32[192,32,2]{1,2,0:T(2,128)S(1)} all-gather(f32[3,32,2]{1,2,0:T(2,128)S(1)} %convert_reduce_fusion), channel_id=3, replica_groups=mesh['grp'=64,'mdl'=8] {'grp'}, dimensions={0}, use_global_device_ids=true | all-gather | bytes 49920 | tf_op jit(solution)/shard_map/all_gather | solution.py:110
  296.5 0.1 copy.107
  296.6 0.2 fusion.24
  296.8 0.1 copy.108
  296.9 0.6 gather_fusion.2
  297.6 0.1 copy.90
  297.8 11.6 %fusion = f32[32,2,128,2]{2,3,1,0:T(2,128)S(1)} fusion(f32[192,32,2,1,128]{4,1,3,2,0:T(8,128)} %all-gather.7.cloned.1.call-done, pred[2,192]{1,0:T(4,128)(4,1)S(1)} %broadcast_compare_fusion.1, f32[2,32,2]{0,2,1:T(2,128)S(1)} %copy.104, f32[192,32,2]{0,2,1:T(2,128)S(1)} %copy.103), kind=kOutput, calls=%fused_computation.3 | convolution fusion | flops 37797888 | bytes 6407040 | tf_op jit(solution)/shard_map/rnqkh,nqkhd->rqkhd/dot_general | solution.py:26
  309.4 0.2 fusion.14
  309.6 0.6 gather_fusion.1
  310.3 0.7 fusion.35
  (43 shorter events, 1.2 us)
Async XLA Ops:
  6.5 25.4 %copy-start = (bf16[4,2048,128]{2,1,0:T(8,128)(2,1)S(1)}, bf16[4,2048,128]{2,1,0:T(8,128)(2,1)}, u32[]{:S(2)}) copy-start(bf16[4,2048,128]{2,1,0:T(8,128)(2,1)} %param.11) | copy-start | bytes 6291460
  6.5 26.7 %copy-start.4 = (s32[192]{0:T(256)S(1)}, s32[192]{0:T(256)}, u32[]{:S(2)}) copy-start(s32[192]{0:T(256)} %param.19) | copy-start | bytes 2308
  6.5 26.8 %copy-start.5 = (s32[3]{0:T(128)S(1)}, s32[3]{0:T(128)}, u32[]{:S(2)}) copy-start(s32[3]{0:T(128)} %param.18) | copy-start | bytes 40
  6.5 121.6 %all-gather.5.cloned.1.call-start = ((), (), s32[]{:S(2)}) async-start(), calls=%async_computation | async-start | bytes 2129920 | tf_op jit(solution)/shard_map/all_gather | solution.py:84
  33.2 264.6 %all-gather.7.cloned.1.call-start = ((), (), s32[]{:S(2)}) async-start(), calls=%async_computation.1 | async-start | bytes 6389760 | tf_op jit(solution)/shard_map/all_gather | solution.py:111
  130.9 3.8 %copy-start.3 = (s32[2,8]{1,0:T(2,128)S(1)}, s32[2,8]{1,0:T(2,128)}, u32[]{:S(2)}) copy-start(s32[2,8]{1,0:T(2,128)} %param.16) | copy-start | bytes 196
  130.9 3.9 %copy-start.2 = (s32[2,32,32]{2,1,0:T(8,128)S(1)}, s32[2,32,32]{2,1,0:T(8,128)}, u32[]{:S(2)}) copy-start(s32[2,32,32]{2,1,0:T(8,128)} %param.15) | copy-start | bytes 24580
  130.9 4.0 %copy-start.1 = (f32[2048,4]{0,1:T(4,128)S(1)}, f32[2048,4]{0,1:T(4,128)}, u32[]{:S(2)}) copy-start(f32[2048,4]{0,1:T(4,128)} %param.13) | copy-start | bytes 98308
Sparse Core Ops, SparseCore 0:
  33.3 94.7 all-gather.4
  134.8 91.8 all-gather.6
where the time goes:
time: 318 us
  blocking collectives  182 us (57%)
  waiting for transfers between devices  94.7 us (30%)
  matrix products  20.8 us (7%)
  between operations  13.6 us (4%)
  local copies, waits for them, and re-layouts  4.98 us (2%)
    all_gather x1, waiting for transfers between devices, on_device(): pieces = lax.all_gather(sending, 'grp', axis=0, tiled=True)  94.7 us
    all_gather x1, blocking collectives, on_device(): lax.all_gather(slot_peak, 'grp', axis=0, tiled=True)  80.5 us
    all_gather x1, blocking collectives, on_device(): lax.all_gather(slot_den, 'grp', axis=0, tiled=True)  77 us
    all_gather x1, blocking collectives, on_device(): pieces = lax.all_gather(draft_hidden, 'mdl', axis=2, tiled=True)  24.4 us
    dot_general x1, matrix products, blend(): jnp.einsum('rnqkh,nqkhd->rqkhd', weight, piece_num, precision=lax.Precisi...  11.6 us
  transfers between devices with their start and end apart: 2, of which 1 were waited for; matrix products, arithmetic and copies ran while one was open for 2% of the time, Pallas kernels for 0%

commit v1 on v0

--- a/solution.py
+++ b/solution.py
@@ -81,7 +81,9 @@
     group_idx = lax.axis_index("grp")
     sending = queries.reshape(requests, query_len, topk_count * head_width)
     my_requests = lax.dynamic_slice_in_dim(slot_request, group_idx * slot_count, slot_count)
-    pieces = lax.all_gather(sending, "grp", axis=0, tiled=True)
+    pieces = jnp.concatenate(
+        lax.all_to_all(jnp.stack([sending] * lax.axis_size("grp")), "grp", 0, 0), axis=0
+    )
     piece_count = pieces.shape[0]
     selector = (my_requests[:, None] == jnp.arange(piece_count, dtype=jnp.int32)[None, :]).astype(
         jnp.bfloat16

time: 318 us -> 309 us (0.972)
  waiting for transfers between devices: 94.7 us -> 52.5 us
  starting transfers between devices: 0.04 us -> 22.5 us
  local copies, waits for them, and re-layouts: 4.98 us -> 16.9 us
    all_gather x1 -> x0, waiting for transfers between devices: 94.7 us -> none  [on_device(): pieces = lax.all_gather(sending, 'grp', axis=0, tiled=True)]
    all_to_all x0 -> x1, waiting for transfers between devices: none -> 52.5 us  [on_device(): lax.all_to_all(jnp.stack([sending] * lax.axis_size('grp')), 'grp', 0, 0)]
    all_to_all x0 -> x1, starting transfers between devices: none -> 22.5 us  [on_device(): lax.all_to_all(jnp.stack([sending] * lax.axis_size('grp')), 'grp', 0, 0)]
    all_to_all x0 -> x1, local copies, waits for them, and re-layouts: none -> 5.06 us  [on_device(): lax.all_to_all(jnp.stack([sending] * lax.axis_size('grp')), 'grp', 0, 0)]
    reshape x0 -> x1, local copies, waits for them, and re-layouts: none -> 4.11 us  [on_device(): jnp.concatenate(lax.all_to_all(jnp.stack([sending] * lax.axis_size('grp')...]
    another operation x1 -> x2, local copies, waits for them, and re-layouts: 0.05 us -> 3.37 us  [the longest x1 3.32 us: on_device(): jnp.stack([sending] * lax.axis_size('grp'))]
where the time goes in v1:
time: 309 us; the launch traced here: 308 us
  blocking collectives  181 us (59%)
  waiting for transfers between devices  52.5 us (17%)
  starting transfers between devices  22.5 us (7%)
  matrix products  20 us (6%)
  local copies, waits for them, and re-layouts  16.9 us (5%)
  between operations  13.6 us (4%)
    all_gather x1, blocking collectives, on_device(): lax.all_gather(slot_peak, 'grp', axis=0, tiled=True)  79.4 us
    all_gather x1, blocking collectives, on_device(): lax.all_gather(slot_den, 'grp', axis=0, tiled=True)  77.2 us
    all_to_all x1, waiting for transfers between devices, on_device(): lax.all_to_all(jnp.stack([sending] * lax.axis_size('grp')), 'grp', 0, 0)  52.5 us
    all_gather x1, blocking collectives, on_device(): pieces = lax.all_gather(draft_hidden, 'mdl', axis=2, tiled=True)  24.4 us
    all_to_all x1, starting transfers between devices, on_device(): lax.all_to_all(jnp.stack([sending] * lax.axis_size('grp')), 'grp', 0, 0)  22.5 us
    dot_general x1, matrix products, blend(): jnp.einsum('rnqkh,nqkhd->rqkhd', weight, piece_num, precision=lax.Precisi...  11.6 us
  transfers between devices with their start and end apart: 2, of which 1 were waited for; matrix products, arithmetic and copies ran while one was open for 2% of the time, Pallas kernels for 0%

profile of v1, /device:TPU:1, one launch (start us, length us, event | category | flops | bytes accessed | tf_op | source)
XLA Modules:
  0.0 308.3 jit_solution(5158137381475810154)
XLA Ops:
  6.5 0.8 copy.88
  7.5 24.4 %all_gather.12 = bf16[2,32,2048]{2,1,0:T(8,128)(2,1)S(1)} all-gather(bf16[2,32,256]{2,1,0:T(8,128)(2,1)} %param.10), channel_id=1, replica_groups=mesh['grp'=64,'mdl'=8] {'mdl'}, dimensions={2}, use_global_device_ids=true | all-gather | bytes 294912 | tf_op jit(solution)/shard_map/all_gather | solution.py:52
  31.9 0.5 fusion.43
  32.4 0.1 select_reduce_fusion
  32.6 3.3 %stack.3 = bf16[64,2,32,256]{3,1,2,0:T(2,128)(2,1)} broadcast(bf16[2,32,256]{2,0,1:T(2,128)(2,1)S(1)} %copy.96), dimensions={1,2,3} | broadcast | bytes 2129920 | tf_op jit(solution)/shard_map/stack | solution.py:85
  36.0 22.5 %all-to-all-start = ((bf16[64,2,32,256]{3,1,2,0:T(2,128)(2,1)}), bf16[64,2,32,256]{3,1,2,0:T(2,128)(2,1)}, u32[]{:S(2)}, u32[]{:S(2)}) async-start(bf16[64,2,32,256]{3,1,2,0:T(2,128)(2,1)} %stack.3), calls=%async_computation | async-start | bytes 4194304 | tf_op jit(solution)/shard_map/all_to_all | solution.py:85
  58.7 52.5 %all-to-all-done = bf16[64,2,32,256]{3,1,2,0:T(2,128)(2,1)} async-done(((bf16[64,2,32,256]{3,1,2,0:T(2,128)(2,1)}), bf16[64,2,32,256]{3,1,2,0:T(2,128)(2,1)}, u32[]{:S(2)}, u32[]{:S(2)}) %all-to-all-start) | async-done | bytes 2097184 | tf_op jit(solution)/shard_map/all_to_all | solution.py:85
  111.2 5.1 %copy.97 = bf16[64,2,32,256]{3,1,0,2:T(2,128)(2,1)} copy(bf16[64,2,32,256]{3,1,2,0:T(2,128)(2,1)} %all-to-all-done) | data formatting | bytes 4194304 | tf_op jit(solution)/shard_map/all_to_all | solution.py:85
  116.2 4.1 %reshape.291 = bf16[128,32,256]{2,0,1:T(8,128)(2,1)} reshape(bf16[64,2,32,256]{3,1,0,2:T(2,128)(2,1)} %copy.97) | data formatting | bytes 4194304 | tf_op jit(solution)/shard_map/reshape | solution.py:84
  120.4 2.0 convolution_convert_fusion
  122.4 1.6 fusion.40
  124.1 2.1 convolution_bitcast_fusion
  126.4 0.3 fusion.42
  126.7 0.1 copy.118
  127.0 0.1 exponential_divide_fusion
  127.2 0.6 gather_fusion
  127.9 1.5 convolution_convert_fusion.1
  129.4 0.2 fusion.41
  129.7 79.4 %all-gather = f32[192,32,2]{1,2,0:T(2,128)S(1)} all-gather(f32[3,32,2]{1,2,0:T(2,128)S(1)} %get-tuple-element.11), channel_id=2, replica_groups=mesh['grp'=64,'mdl'=8] {'grp'}, dimensions={0}, use_global_device_ids=true | all-gather | bytes 49920 | tf_op jit(solution)/shard_map/all_gather | solution.py:111
  209.1 0.1 copy.101
  209.2 0.1 copy.105
  209.3 0.1 select_reduce_fusion.1
  209.5 0.1 copy.106
  209.6 0.3 convert_reduce_fusion
  209.8 77.2 %all-gather.1 = f32[192,32,2]{1,2,0:T(2,128)S(1)} all-gather(f32[3,32,2]{1,2,0:T(2,128)S(1)} %convert_reduce_fusion), channel_id=3, replica_groups=mesh['grp'=64,'mdl'=8] {'grp'}, dimensions={0}, use_global_device_ids=true | all-gather | bytes 49920 | tf_op jit(solution)/shard_map/all_gather | solution.py:112
  287.0 0.1 copy.109
  287.1 0.2 fusion.19
  287.4 0.6 gather_fusion.2
  288.3 11.6 %fusion = f32[32,2,128,2]{2,3,1,0:T(2,128)S(1)} fusion(f32[192,32,2,1,128]{4,1,3,2,0:T(8,128)} %all-gather.4.cloned.1.call-done, pred[2,192]{1,0:T(4,128)(4,1)S(1)} %broadcast_compare_fusion.1, f32[2,32,2]{0,2,1:T(2,128)S(1)} %copy.106, f32[192,32,2]{0,2,1:T(2,128)S(1)} %copy.105), kind=kOutput, calls=%fused_computation.3 | convolution fusion | flops 37797888 | bytes 6407040 | tf_op jit(solution)/shard_map/rnqkh,nqkhd->rqkhd/dot_general | solution.py:26
  299.9 0.2 fusion.9
  300.2 0.6 gather_fusion.1
  300.8 0.7 fusion.30
  (46 shorter events, 1.6 us)
Async XLA Ops:
  6.5 25.4 %copy-start = (bf16[4,2048,128]{2,1,0:T(8,128)(2,1)S(1)}, bf16[4,2048,128]{2,1,0:T(8,128)(2,1)}, u32[]{:S(2)}) copy-start(bf16[4,2048,128]{2,1,0:T(8,128)(2,1)} %param.11) | copy-start | bytes 6291460
  36.0 22.5 %copy-start.4 = (s32[192]{0:T(256)S(1)}, s32[192]{0:T(256)}, u32[]{:S(2)}) copy-start(s32[192]{0:T(256)} %param.19) | copy-start | bytes 2308
  36.0 22.6 %copy-start.5 = (s32[3]{0:T(128)S(1)}, s32[3]{0:T(128)}, u32[]{:S(2)}) copy-start(s32[3]{0:T(128)} %param.18) | copy-start | bytes 40
  36.0 75.2 %all-to-all-start = ((bf16[64,2,32,256]{3,1,2,0:T(2,128)(2,1)}), bf16[64,2,32,256]{3,1,2,0:T(2,128)(2,1)}, u32[]{:S(2)}, u32[]{:S(2)}) async-start(bf16[64,2,32,256]{3,1,2,0:T(2,128)(2,1)} %stack.3), calls=%async_computation | async-start | bytes 4194304 | tf_op jit(solution)/shard_map/all_to_all | solution.py:85
  58.4 229.9 %all-gather.4.cloned.1.call-start = ((), (), s32[]{:S(2)}) async-start(), calls=%async_computation.1 | async-start | bytes 6389760 | tf_op jit(solution)/shard_map/all_gather | solution.py:113
  122.4 3.8 %copy-start.3 = (s32[2,8]{1,0:T(2,128)S(1)}, s32[2,8]{1,0:T(2,128)}, u32[]{:S(2)}) copy-start(s32[2,8]{1,0:T(2,128)} %param.16) | copy-start | bytes 196
  122.4 3.9 %copy-start.2 = (s32[2,32,32]{2,1,0:T(8,128)S(1)}, s32[2,32,32]{2,1,0:T(8,128)}, u32[]{:S(2)}) copy-start(s32[2,32,32]{2,1,0:T(8,128)} %param.15) | copy-start | bytes 24580
  122.4 4.0 %copy-start.1 = (f32[2048,4]{0,1:T(4,128)S(1)}, f32[2048,4]{0,1:T(4,128)}, u32[]{:S(2)}) copy-start(f32[2048,4]{0,1:T(4,128)} %param.13) | copy-start | bytes 98308
Sparse Core Ops, SparseCore 0:
  126.3 98.3 all-gather.3
